TPU v7x, 512 devices: a whole 4x4x16 slice. The times are simulated.
512 devices in a mesh: gx: 64 (over z, y), gy: 8 (over x, core).
Axes of the slice: x: 4, y: 4, z: 16, core: 2. Of those that a mesh axis runs over, the one named last changes fastest.
Arguments:
- rhs: float32 [64, 8, 128, 128], P('gx', 'gy'), may hold values from -57 to 57
- face_rows: int32 [64, 8, 4, 128], P('gx', 'gy'), may hold values from 0 to 127
- margin_weight: float32 [64, 8, 4, 128], P('gx', 'gy'), may hold values from 0.2 to 1
- local_blocks: bfloat16 [64, 8, 1, 128, 128], P('gx', 'gy'), may hold values from -0.4 to 4.4
- subdomain_inverse: bfloat16 [64, 8, 128, 640], P('gx', 'gy'), may hold values from -0.4 to 1.8
- coarse_basis: bfloat16 [64, 8, 128, 32], P('gx', 'gy'), may hold values from -0.5 to 0.5
- coarse_inverse: bfloat16 [64, 8, 32, 16384], P('gx', 'gy'), may hold values from -0.09765625 to 0.09765625
- coarse_map: int32 [512], replicated, may hold values from 0 to 511, each once
Outputs:
- solution: float32 [64, 8, 128, 128], P('gx', 'gy')
- relative_residual: float32 [128], replicated
Inputs may be any that keep to these rules, and one draw needn't show every extreme that they name: `face_rows`: rows of the subdomain, repeats possible. `coarse_map`: every position once.
All inputs are finite; a program needn't handle non-finite values.
Results may differ from a plain program's by a relative error of at most 0.004.
Values may be sent and summed in bfloat16 or wider, within the bound.
No kernel may reach another device: no remote copies, remote signals or barrier semaphores. Data moves between devices by JAX's collectives and lax.ppermute only.
A program may use at most 64 MiB of HBM per device.

v0:
```python
import jax
import jax.numpy as jnp
from jax import lax
from jax.sharding import PartitionSpec as P

EPSILON = 1e-06


def padded(shard, sides, width):
    for axis, dim in sides:
        count, length = (lax.axis_size(axis), shard.shape[dim])
        up = [(i, (i + 1) % count) for i in range(count - 1)]
        down = [(j, i) for i, j in up]
        last = lax.slice_in_dim(shard, length - width, length, axis=dim)
        initial = lax.slice_in_dim(shard, 0, width, axis=dim)
        before = lax.ppermute(last, axis, up)
        after = lax.ppermute(initial, axis, down)
        shard = jnp.concatenate([before, shard, after], axis=dim)
    return shard


def least_squares(scale_norm, first_dot, first_norm, cross_dot, second_dot, second_norm):
    radius_one = jnp.sqrt(first_dot * first_dot + first_norm * first_norm)
    cosine_one = first_dot / radius_one
    sine_one = first_norm / radius_one
    upper_entry = cosine_one * cross_dot + sine_one * second_dot
    lower_entry = cosine_one * second_dot - sine_one * cross_dot
    radius_two = jnp.sqrt(lower_entry * lower_entry + second_norm * second_norm)
    cosine_two = lower_entry / radius_two
    sine_two = second_norm / radius_two
    weight_two = -cosine_two * sine_one * scale_norm / radius_two
    weight_one = (cosine_one * scale_norm - upper_entry * weight_two) / radius_one
    return (weight_one, weight_two, sine_one * sine_two)


def on_device(
    rhs,
    face_rows,
    margin_weight,
    local_blocks,
    subdomain_inverse,
    coarse_basis,
    coarse_inverse,
    coarse_map,
):
    right_side = rhs[0, 0]
    margin_rows = face_rows[0, 0]
    margin_weights = margin_weight[0, 0]
    local_block = local_blocks[0, 0]
    inverse_rows = subdomain_inverse[0, 0]
    basis = coarse_basis[0, 0]
    coarse_rows = coarse_inverse[0, 0]
    owned_rows = right_side.shape[0]
    system_count = right_side.shape[1]
    basis_count = basis.shape[1]
    block_rows = local_block.shape[1]
    positions = (
        coarse_map[:, None] * basis_count + jnp.arange(basis_count, dtype=jnp.int32)[None, :]
    ).reshape(-1)
    permuted = jnp.take(coarse_rows, positions, axis=1)

    def neighbour_margin(rounded):
        face_packs = rounded[margin_rows]
        along_first = padded(face_packs[0:2], (("gx", 0),), 1)
        along_second = padded(face_packs[2:4], (("gy", 0),), 1)
        return jnp.stack([along_first[0], along_first[3], along_second[0], along_second[3]], axis=0)

    def add_piece(shard_rows):
        return jnp.dot(permuted, shard_rows, preferred_element_type=jnp.float32)

    def precondition(vector):
        rounded = vector.astype(jnp.bfloat16)
        extended = jnp.concatenate(
            [rounded, neighbour_margin(rounded).reshape(-1, system_count)], axis=0
        )
        local_part = jnp.dot(inverse_rows, extended, preferred_element_type=jnp.float32)
        residual = lax.dot_general(
            basis, rounded, (((0,), (0,)), ((), ())), preferred_element_type=jnp.float32
        ).astype(jnp.bfloat16)
        solved = add_piece(lax.all_gather(residual, ("gx", "gy"), axis=0, tiled=True))
        return local_part + jnp.dot(
            basis, solved.astype(jnp.bfloat16), preferred_element_type=jnp.float32
        )

    def apply_operator(vector):
        rounded = vector.astype(jnp.bfloat16)
        own_part = jnp.einsum(
            "brc,bcn->brn",
            local_block,
            rounded.reshape(-1, block_rows, system_count),
            preferred_element_type=jnp.float32,
        ).reshape(owned_rows, system_count)
        weighted = margin_weights[:, :, None] * neighbour_margin(rounded).astype(jnp.float32)
        coupling = (
            jnp.zeros((owned_rows, system_count), jnp.float32)
            .at[margin_rows.reshape(-1)]
            .add(weighted.reshape(-1, system_count))
        )
        return own_part - coupling

    def column_norm(vector):
        squares = lax.psum(jnp.sum(vector * vector, axis=0), ("gx", "gy"))
        return jnp.sqrt(squares + EPSILON)

    def project_single(vector, direction):
        return lax.psum(jnp.sum(vector * direction, axis=0), ("gx", "gy"))

    scale_norm = column_norm(right_side)
    krylov_one = right_side / scale_norm
    precond_one = precondition(krylov_one)
    applied = apply_operator(precond_one)
    first_dot = project_single(applied, krylov_one)
    remainder = applied - first_dot * krylov_one
    first_norm = column_norm(remainder)
    krylov_two = remainder / first_norm
    precond_two = precondition(krylov_two)
    applied = apply_operator(precond_two)
    cross_dot = project_single(applied, krylov_one)
    remainder = applied - cross_dot * krylov_one
    second_dot = project_single(remainder, krylov_two)
    remainder = remainder - second_dot * krylov_two
    second_norm = column_norm(remainder)
    weight_one, weight_two, relative = least_squares(
        scale_norm, first_dot, first_norm, cross_dot, second_dot, second_norm
    )
    solution = weight_one * precond_one + weight_two * precond_two
    return (solution[None, None], relative)


def solution(mesh):
    return jax.shard_map(
        on_device,
        mesh=mesh,
        in_specs=(
            P("gx", "gy", None, None),
            P("gx", "gy", None, None),
            P("gx", "gy", None, None),
            P("gx", "gy", None, None, None),
            P("gx", "gy", None, None),
            P("gx", "gy", None, None),
            P("gx", "gy", None, None),
            P(),
        ),
        out_specs=(P("gx", "gy", None, None), P()),
        check_vma=False,
    )
```

profile of v0, /device:TPU:1, one launch (start us, length us, event | category | flops | bytes accessed | tf_op | source)
XLA Modules:
  0.0 1066.4 jit_solution(7111828778543676201)
XLA Ops:
  8.1 111.0 %psum.42 = f32[128]{0:T(128)S(1)} all-reduce(f32[128]{0:T(128)S(1)} %fusion.22), channel_id=1, replica_groups=mesh['gx'=64,'gy'=8] {'gx','gy'}, use_global_device_ids=true, to_apply=%region_1.2 | all-reduce | flops 128 | bytes 1024 | tf_op jit(solution)/shard_map/psum | solution.py:102
  119.1 1.6 fusion.6
  125.0 3.3 collective-permute-start.2
  129.6 1.9 collective-permute-start.3
  132.8 4.6 copy.18
  137.4 57.6 %gather_fusion.1 = bf16[16384,32]{1,0:T(8,128)(2,1)} fusion(bf16[32,16384]{0,1:T(8,128)(2,1)} %bitcast.121, s32[16384]{0:T(1024)S(1)} %broadcast_clamp_fusion), kind=kCustom, calls=%fused_computation.1 | custom fusion | bytes 2162688 | tf_op jit(solution)/shard_map/jit(_take)/gather | solution.py:60
  195.4 117.2 %all-gather.3.cloned.1.call-done = bf16[16384,128]{1,0:T(8,128)(2,1)} async-done(((bf16[32,128]{1,0:T(8,128)(2,1)}), bf16[16384,128]{1,0:T(8,128)(2,1)}) %all-gather.3.cloned.1.call-update) | async-done | bytes 4194320 | tf_op jit(solution)/shard_map/all_gather | solution.py:80
  312.7 7.1 convolution_add_fusion.1
  319.9 1.3 gather_fusion.2
  321.2 3.4 collective-permute-start.4
  324.6 3.6 collective-permute-start.6
  329.5 1.9 collective-permute-start.7
  331.5 1.4 collective-permute-done.5
  332.9 1.9 collective-permute-done.7
  334.8 2.4 scatter_custom_fusion
  337.4 102.7 %psum.43 = f32[128]{0:T(128)S(1)} all-reduce(f32[128]{0:T(128)S(1)} %get-tuple-element.29), channel_id=1, replica_groups=mesh['gx'=64,'gy'=8] {'gx','gy'}, use_global_device_ids=true, to_apply=%region_4.5 | all-reduce | flops 128 | bytes 1024 | tf_op jit(solution)/shard_map/psum | solution.py:106
  440.2 98.7 %psum.44 = f32[128]{0:T(128)S(1)} all-reduce(f32[128]{0:T(128)S(1)} %multiply_reduce_fusion.3), channel_id=1, replica_groups=mesh['gx'=64,'gy'=8] {'gx','gy'}, use_global_device_ids=true, to_apply=%region_6.7 | all-reduce | flops 128 | bytes 1024 | tf_op jit(solution)/shard_map/psum | solution.py:102
  541.1 2.4 collective-permute-start.8
  543.4 1.9 collective-permute-start.10
  546.7 2.6 collective-permute-start.11
  552.2 180.1 %all-gather.5.cloned.1.call-done = bf16[16384,128]{1,0:T(8,128)(2,1)} async-done(((bf16[32,128]{1,0:T(8,128)(2,1)}), bf16[16384,128]{1,0:T(8,128)(2,1)}) %all-gather.5.cloned.1.call-update) | async-done | bytes 4194320 | tf_op jit(solution)/shard_map/all_gather | solution.py:80
  732.2 7.1 convolution_add_fusion
  739.4 1.3 gather_fusion.4
  740.8 3.4 collective-permute-start.12
  744.2 3.6 collective-permute-start.14
  749.1 1.9 collective-permute-start.15
  751.1 1.4 collective-permute-done.13
  752.5 1.9 collective-permute-done.15
  754.4 2.4 scatter_custom_fusion.1
  757.0 102.7 %psum.45 = f32[128]{0:T(128)S(1)} all-reduce(f32[128]{0:T(128)S(1)} %get-tuple-element.31), channel_id=1, replica_groups=mesh['gx'=64,'gy'=8] {'gx','gy'}, use_global_device_ids=true, to_apply=%region_9.10 | all-reduce | flops 128 | bytes 1024 | tf_op jit(solution)/shard_map/psum | solution.py:106
  859.8 98.7 %psum.46 = f32[128]{0:T(128)S(1)} all-reduce(f32[128]{0:T(128)S(1)} %multiply_reduce_fusion.1), channel_id=1, replica_groups=mesh['gx'=64,'gy'=8] {'gx','gy'}, use_global_device_ids=true, to_apply=%region_11.12 | all-reduce | flops 128 | bytes 1024 | tf_op jit(solution)/shard_map/psum | solution.py:106
  958.5 99.6 %psum.47 = f32[128]{0:T(128)S(1)} all-reduce(f32[128]{0:T(128)S(1)} %multiply_reduce_fusion), channel_id=1, replica_groups=mesh['gx'=64,'gy'=8] {'gx','gy'}, use_global_device_ids=true, to_apply=%region_13.14 | all-reduce | flops 128 | bytes 1024 | tf_op jit(solution)/shard_map/psum | solution.py:102
  (74 shorter events, 19.1 us)
Async XLA Ops:
  7.2 187.9 %copy-start = (bf16[1,1,128,640]{3,2,1,0:T(8,128)(2,1)S(1)}, bf16[1,1,128,640]{3,2,1,0:T(8,128)(2,1)}, u32[]{:S(2)}) copy-start(bf16[1,1,128,640]{3,2,1,0:T(8,128)(2,1)} %param.12) | copy-start | bytes 491524
  7.2 305.5 %all-gather.3.cloned.1.call-start = ((), (), s32[]{:S(2)}) async-start(), calls=%async_computation | async-start | bytes 4202496 | tf_op jit(solution)/shard_map/all_gather | solution.py:80
  120.8 611.5 %all-gather.5.cloned.1.call-start = ((), (), s32[]{:S(2)}) async-start(), calls=%async_computation.1 | async-start | bytes 4202496 | tf_op jit(solution)/shard_map/all_gather | solution.py:80
  123.7 71.3 %collective-permute-start = (bf16[1,128,128]{2,1,0:T(8,128)(2,1)S(1)}, bf16[1,128,128]{2,1,0:T(8,128)(2,1)S(1)}, u32[]{:S(2)}, u32[]{:S(2)}) collective-permute-start(bf16[1,128,128]{2,1,0:T(8,128)(2,1)S(1)} %get-tuple-element.25), channel_id=1, source_target_pairs={{0,8},{8,16},{16,24},{24,32},{32,40},{40,48},{48,56},{56,64},{64,7... | collective-permute-start | bytes 98312 | tf_op jit(solution)/shard_map/ppermute | solution.py:16
  125.0 70.0 %collective-permute-start.2 = (bf16[1,128,128]{2,1,0:T(8,128)(2,1)S(1)}, bf16[1,128,128]{2,1,0:T(8,128)(2,1)S(1)}, u32[]{:S(2)}, u32[]{:S(2)}) collective-permute-start(bf16[1,128,128]{2,1,0:T(8,128)(2,1)S(1)} %get-tuple-element.26), channel_id=1, source_target_pairs={{0,1},{1,2},{2,3},{3,4},{4,5},{5,6},{6,7},{8,9},{9,10},{10,11},{11... | collective-permute-start | bytes 98312 | tf_op jit(solution)/shard_map/ppermute | solution.py:16
  128.3 66.7 %collective-permute-start.1 = (bf16[1,128,128]{2,1,0:T(8,128)(2,1)S(1)}, bf16[1,128,128]{2,1,0:T(8,128)(2,1)S(1)}, u32[]{:S(2)}, u32[]{:S(2)}) collective-permute-start(bf16[1,128,128]{2,1,0:T(8,128)(2,1)S(1)} %get-tuple-element.27), channel_id=1, source_target_pairs={{8,0},{16,8},{24,16},{32,24},{40,32},{48,40},{56,48},{64,56},{72,6... | collective-permute-start | bytes 98312 | tf_op jit(solution)/shard_map/ppermute | solution.py:17
  129.6 65.4 %collective-permute-start.3 = (bf16[1,128,128]{2,1,0:T(8,128)(2,1)S(1)}, bf16[1,128,128]{2,1,0:T(8,128)(2,1)S(1)}, u32[]{:S(2)}, u32[]{:S(2)}) collective-permute-start(bf16[1,128,128]{2,1,0:T(8,128)(2,1)S(1)} %get-tuple-element.28), channel_id=1, source_target_pairs={{1,0},{2,1},{3,2},{4,3},{5,4},{6,5},{7,6},{9,8},{10,9},{11,10},{12... | collective-permute-start | bytes 98312 | tf_op jit(solution)/shard_map/ppermute | solution.py:17
  137.4 175.2 %copy-start.5 = (bf16[1,1,128,32]{2,3,1,0:T(8,128)(2,1)S(1)}, bf16[1,1,128,32]{2,3,1,0:T(8,128)(2,1)}, u32[]{:S(2)}) copy-start(bf16[1,1,128,32]{2,3,1,0:T(8,128)(2,1)} %param.13) | copy-start | bytes 24580
  195.4 136.1 %copy-start.4 = (s32[1,1,4,128]{3,2,1,0:T(4,128)S(1)}, s32[1,1,4,128]{3,2,1,0:T(4,128)}, u32[]{:S(2)}) copy-start(s32[1,1,4,128]{3,2,1,0:T(4,128)} %param.9) | copy-start | bytes 6148
  195.4 139.4 %copy-start.3 = (f32[1,1,4,128]{3,2,1,0:T(4,128)S(1)}, f32[1,1,4,128]{3,2,1,0:T(4,128)}, u32[]{:S(2)}) copy-start(f32[1,1,4,128]{3,2,1,0:T(4,128)} %param.10) | copy-start | bytes 6148
  195.4 141.8 %copy-start.1 = (f32[1,1,128,128]{3,2,1,0:T(8,128)S(1)}, f32[1,1,128,128]{3,2,1,0:T(8,128)}, u32[]{:S(2)}) copy-start(f32[1,1,128,128]{3,2,1,0:T(8,128)} %param.8) | copy-start | bytes 196612
  195.4 141.8 %copy-start.2 = (bf16[1,1,1,128,128]{4,3,2,1,0:T(8,128)(2,1)S(1)}, bf16[1,1,1,128,128]{4,3,2,1,0:T(8,128)(2,1)}, u32[]{:S(2)}) copy-start(bf16[1,1,1,128,128]{4,3,2,1,0:T(8,128)(2,1)} %param.11) | copy-start | bytes 98308
  321.2 10.3 collective-permute-start.4
  324.6 6.9 collective-permute-start.6
  328.2 4.7 collective-permute-start.5
  329.5 5.2 collective-permute-start.7
  541.1 8.2 collective-permute-start.8
  543.4 5.8 collective-permute-start.10
  545.4 5.2 collective-permute-start.9
  546.7 5.2 collective-permute-start.11
  740.8 10.2 collective-permute-start.12
  744.2 6.8 collective-permute-start.14
  747.8 4.7 collective-permute-start.13
  749.1 5.2 collective-permute-start.15
Sparse Core Ops, SparseCore 0:
  120.9 191.7 all-gather.2
  539.8 192.3 all-gather.4
where the time goes:
time: 1070 us
  blocking collectives  614 us (57%)
  waiting for transfers between devices  307 us (29%)
  local copies, waits for them, and re-layouts  68.9 us (6%)
  starting transfers between devices  36.5 us (3%)
  matrix products  17.3 us (2%)
  between operations  14.5 us (1%)
    psum x3, blocking collectives, column_norm(): squares = lax.psum(jnp.sum(vector * vector, axis=0), ('gx', 'gy'))  309 us
    psum x3, blocking collectives, project_single(): return lax.psum(jnp.sum(vector * direction, axis=0), ('gx', 'gy'))  304 us
    all_gather x2, waiting for transfers between devices, precondition(): lax.all_gather(residual, ('gx', 'gy'), axis=0, tiled=True)  297 us
    gather x1, local copies, waits for them, and re-layouts, on_device(): permuted = jnp.take(coarse_rows, positions, axis=1)  57.6 us
    ppermute x8, starting transfers between devices, padded(): before = lax.ppermute(last, axis, up)  22.9 us
  transfers between devices with their start and end apart: 18, of which 8 were waited for; matrix products, arithmetic and copies ran while one was open for 6% of the time, Pallas kernels for 0%

commit v1 on v0

--- a/solution.py
+++ b/solution.py
@@ -77,7 +77,14 @@
         residual = lax.dot_general(
             basis, rounded, (((0,), (0,)), ((), ())), preferred_element_type=jnp.float32
         ).astype(jnp.bfloat16)
-        solved = add_piece(lax.all_gather(residual, ("gx", "gy"), axis=0, tiled=True))
+        solved = add_piece(
+            jnp.concatenate(
+                lax.all_to_all(
+                    jnp.stack([residual] * lax.axis_size(("gx", "gy"))), ("gx", "gy"), 0, 0
+                ),
+                axis=0,
+            )
+        )
         return local_part + jnp.dot(
             basis, solved.astype(jnp.bfloat16), preferred_element_type=jnp.float32
         )

time: 1070 us -> 1080 us (level)
  starting transfers between devices: 36.5 us -> 68 us
  between operations: 14.5 us -> 1.17 us
    all_gather x2 -> x0, waiting for transfers between devices: 297 us -> none  [precondition(): lax.all_gather(residual, ('gx', 'gy'), axis=0, tiled=True)]
    all_to_all x0 -> x2, waiting for transfers between devices: none -> 286 us  [precondition(): lax.all_to_all(jnp.stack([residual] * lax.axis_size(('gx', 'gy'))), ('gx'...]
    all_to_all x0 -> x2, starting transfers between devices: none -> 27.4 us  [precondition(): lax.all_to_all(jnp.stack([residual] * lax.axis_size(('gx', 'gy'))), ('gx'...]
where the time goes in v1:
time: 1080 us; the launch traced here: 1070 us
  blocking collectives  613 us (57%)
  waiting for transfers between devices  297 us (28%)
  local copies, waits for them, and re-layouts  72.5 us (7%)
  starting transfers between devices  68 us (6%)
  matrix products  16.1 us (1%)
    psum x3, blocking collectives, column_norm(): squares = lax.psum(jnp.sum(vector * vector, axis=0), ('gx', 'gy'))  309 us
    psum x3, blocking collectives, project_single(): return lax.psum(jnp.sum(vector * direction, axis=0), ('gx', 'gy'))  304 us
    all_to_all x2, waiting for transfers between devices, precondition(): lax.all_to_all(jnp.stack([residual] * lax.axis_size(('gx', 'gy'))), ('gx'...  286 us
    gather x1, local copies, waits for them, and re-layouts, on_device(): permuted = jnp.take(coarse_rows, positions, axis=1)  57.6 us
    ppermute x8, starting transfers between devices, padded(): before = lax.ppermute(last, axis, up)  27.7 us
    all_to_all x2, starting transfers between devices, precondition(): lax.all_to_all(jnp.stack([residual] * lax.axis_size(('gx', 'gy'))), ('gx'...  27.4 us
  transfers between devices with their start and end apart: 18, of which 8 were waited for; matrix products, arithmetic and copies ran while one was open for 6% of the time, Pallas kernels for 0%

profile of v1, /device:TPU:1, one launch (start us, length us, event | category | flops | bytes accessed | tf_op | source)
XLA Modules:
  0.0 1074.9 jit_solution(7648320048224804574)
XLA Ops:
  1.6 111.0 %psum.42 = f32[128]{0:T(128)S(1)} all-reduce(f32[128]{0:T(128)S(1)} %fusion.22), channel_id=1, replica_groups=mesh['gx'=64,'gy'=8] {'gx','gy'}, use_global_device_ids=true, to_apply=%region_1.2 | all-reduce | flops 128 | bytes 1024 | tf_op jit(solution)/shard_map/psum | solution.py:109
  113.6 2.5 stack.13
  116.1 14.2 %all-to-all-start = ((bf16[512,32,128]{2,1,0:T(8,128)(2,1)}), bf16[512,32,128]{2,1,0:T(8,128)(2,1)}, u32[]{:S(2)}, u32[]{:S(2)}) async-start(bf16[512,32,128]{2,1,0:T(8,128)(2,1)} %stack.13), calls=%async_computation | async-start | bytes 8388608 | tf_op jit(solution)/shard_map/all_to_all | solution.py:82
  131.7 3.3 collective-permute-start
  135.0 3.7 collective-permute-start.2
  139.9 2.0 collective-permute-start.3
  142.5 3.2 copy.14
  145.7 57.6 %gather_fusion.1 = bf16[16384,32]{1,0:T(8,128)(2,1)} fusion(bf16[32,16384]{0,1:T(8,128)(2,1)} %bitcast.123, s32[16384]{0:T(1024)S(1)} %broadcast_clamp_fusion), kind=kCustom, calls=%fused_computation.1 | custom fusion | bytes 2162688 | tf_op jit(solution)/shard_map/jit(_take)/gather | solution.py:60
  203.6 114.5 %all-to-all-done = bf16[512,32,128]{2,1,0:T(8,128)(2,1)} async-done(((bf16[512,32,128]{2,1,0:T(8,128)(2,1)}), bf16[512,32,128]{2,1,0:T(8,128)(2,1)}, u32[]{:S(2)}, u32[]{:S(2)}) %all-to-all-start) | async-done | bytes 4194336 | tf_op jit(solution)/shard_map/all_to_all | solution.py:82
  318.0 7.1 convolution_add_fusion.1
  326.6 3.2 collective-permute-start.4
  329.8 3.8 collective-permute-start.6
  336.8 2.0 collective-permute-done.5
  340.2 2.4 scatter_custom_fusion
  342.7 103.0 %psum.43 = f32[128]{0:T(128)S(1)} all-reduce(f32[128]{0:T(128)S(1)} %get-tuple-element.27), channel_id=1, replica_groups=mesh['gx'=64,'gy'=8] {'gx','gy'}, use_global_device_ids=true, to_apply=%region_4.5 | all-reduce | flops 128 | bytes 1024 | tf_op jit(solution)/shard_map/psum | solution.py:113
  445.8 98.4 %psum.44 = f32[128]{0:T(128)S(1)} all-reduce(f32[128]{0:T(128)S(1)} %multiply_reduce_fusion.3), channel_id=1, replica_groups=mesh['gx'=64,'gy'=8] {'gx','gy'}, use_global_device_ids=true, to_apply=%region_6.7 | all-reduce | flops 128 | bytes 1024 | tf_op jit(solution)/shard_map/psum | solution.py:109
  544.3 2.5 stack.16
  546.8 13.2 %all-to-all-start.1 = ((bf16[512,32,128]{2,1,0:T(8,128)(2,1)}), bf16[512,32,128]{2,1,0:T(8,128)(2,1)}, u32[]{:S(2)}, u32[]{:S(2)}) async-start(bf16[512,32,128]{2,1,0:T(8,128)(2,1)} %stack.16), calls=%async_computation.1 | async-start | bytes 8388608 | tf_op jit(solution)/shard_map/all_to_all | solution.py:82
  561.4 3.3 collective-permute-start.8
  564.7 3.7 collective-permute-start.10
  569.6 2.0 collective-permute-start.11
  571.6 2.0 collective-permute-done.9
  573.6 2.0 collective-permute-done.11
  575.8 172.0 %all-to-all-done.1 = bf16[512,32,128]{2,1,0:T(8,128)(2,1)} async-done(((bf16[512,32,128]{2,1,0:T(8,128)(2,1)}), bf16[512,32,128]{2,1,0:T(8,128)(2,1)}, u32[]{:S(2)}, u32[]{:S(2)}) %all-to-all-start.1) | async-done | bytes 4194336 | tf_op jit(solution)/shard_map/all_to_all | solution.py:82
  747.8 7.1 convolution_add_fusion
  756.4 3.2 collective-permute-start.12
  759.6 3.8 collective-permute-start.14
  766.6 2.0 collective-permute-done.13
  769.9 2.4 scatter_custom_fusion.1
  772.5 102.8 %psum.45 = f32[128]{0:T(128)S(1)} all-reduce(f32[128]{0:T(128)S(1)} %get-tuple-element.29), channel_id=1, replica_groups=mesh['gx'=64,'gy'=8] {'gx','gy'}, use_global_device_ids=true, to_apply=%region_9.10 | all-reduce | flops 128 | bytes 1024 | tf_op jit(solution)/shard_map/psum | solution.py:113
  875.3 98.4 %psum.46 = f32[128]{0:T(128)S(1)} all-reduce(f32[128]{0:T(128)S(1)} %multiply_reduce_fusion.1), channel_id=1, replica_groups=mesh['gx'=64,'gy'=8] {'gx','gy'}, use_global_device_ids=true, to_apply=%region_11.12 | all-reduce | flops 128 | bytes 1024 | tf_op jit(solution)/shard_map/psum | solution.py:113
  973.8 99.7 %psum.47 = f32[128]{0:T(128)S(1)} all-reduce(f32[128]{0:T(128)S(1)} %multiply_reduce_fusion), channel_id=1, replica_groups=mesh['gx'=64,'gy'=8] {'gx','gy'}, use_global_device_ids=true, to_apply=%region_13.14 | all-reduce | flops 128 | bytes 1024 | tf_op jit(solution)/shard_map/psum | solution.py:109
  (78 shorter events, 22.4 us)
Async XLA Ops:
  0.6 202.7 %copy-start = (bf16[1,1,128,640]{3,2,1,0:T(8,128)(2,1)S(1)}, bf16[1,1,128,640]{3,2,1,0:T(8,128)(2,1)}, u32[]{:S(2)}) copy-start(bf16[1,1,128,640]{3,2,1,0:T(8,128)(2,1)} %param.12) | copy-start | bytes 491524
  116.1 14.2 %copy-start.5 = (s32[1,1,4,128]{3,2,1,0:T(4,128)S(1)}, s32[1,1,4,128]{3,2,1,0:T(4,128)}, u32[]{:S(2)}) copy-start(s32[1,1,4,128]{3,2,1,0:T(4,128)} %param.9) | copy-start | bytes 6148
  116.1 14.2 %copy-start.1 = (f32[1,1,128,128]{3,2,1,0:T(8,128)S(1)}, f32[1,1,128,128]{3,2,1,0:T(8,128)}, u32[]{:S(2)}) copy-start(f32[1,1,128,128]{3,2,1,0:T(8,128)} %param.8) | copy-start | bytes 196612
  116.1 25.8 %copy-start.7 = (s32[512]{0:T(512)S(1)}, s32[512]{0:T(512)}, u32[]{:S(2)}) copy-start(s32[512]{0:T(512)} %param.15) | copy-start | bytes 6148
  116.1 26.4 %copy-start.2 = (bf16[1,1,32,16384]{3,2,1,0:T(8,128)(2,1)S(1)}, bf16[1,1,32,16384]{3,2,1,0:T(8,128)(2,1)}, u32[]{:S(2)}) copy-start(bf16[1,1,32,16384]{3,2,1,0:T(8,128)(2,1)} %param.14) | copy-start | bytes 3145732
  116.1 201.9 %all-to-all-start = ((bf16[512,32,128]{2,1,0:T(8,128)(2,1)}), bf16[512,32,128]{2,1,0:T(8,128)(2,1)}, u32[]{:S(2)}, u32[]{:S(2)}) async-start(bf16[512,32,128]{2,1,0:T(8,128)(2,1)} %stack.13), calls=%async_computation | async-start | bytes 8388608 | tf_op jit(solution)/shard_map/all_to_all | solution.py:82
  131.7 71.6 %collective-permute-start = (bf16[1,128,128]{2,1,0:T(8,128)(2,1)S(1)}, bf16[1,128,128]{2,1,0:T(8,128)(2,1)S(1)}, u32[]{:S(2)}, u32[]{:S(2)}) collective-permute-start(bf16[1,128,128]{2,1,0:T(8,128)(2,1)S(1)} %get-tuple-element.23), channel_id=1, source_target_pairs={{0,8},{8,16},{16,24},{24,32},{32,40},{40,48},{48,56},{56,64},{64,7... | collective-permute-start | bytes 98312 | tf_op jit(solution)/shard_map/ppermute | solution.py:16
  135.0 68.3 %collective-permute-start.2 = (bf16[1,128,128]{2,1,0:T(8,128)(2,1)S(1)}, bf16[1,128,128]{2,1,0:T(8,128)(2,1)S(1)}, u32[]{:S(2)}, u32[]{:S(2)}) collective-permute-start(bf16[1,128,128]{2,1,0:T(8,128)(2,1)S(1)} %get-tuple-element.24), channel_id=1, source_target_pairs={{0,1},{1,2},{2,3},{3,4},{4,5},{5,6},{6,7},{8,9},{9,10},{10,11},{11... | collective-permute-start | bytes 98312 | tf_op jit(solution)/shard_map/ppermute | solution.py:16
  138.6 64.6 %collective-permute-start.1 = (bf16[1,128,128]{2,1,0:T(8,128)(2,1)S(1)}, bf16[1,128,128]{2,1,0:T(8,128)(2,1)S(1)}, u32[]{:S(2)}, u32[]{:S(2)}) collective-permute-start(bf16[1,128,128]{2,1,0:T(8,128)(2,1)S(1)} %get-tuple-element.25), channel_id=1, source_target_pairs={{8,0},{16,8},{24,16},{32,24},{40,32},{48,40},{56,48},{64,56},{72,6... | collective-permute-start | bytes 98312 | tf_op jit(solution)/shard_map/ppermute | solution.py:17
  139.9 63.3 %collective-permute-start.3 = (bf16[1,128,128]{2,1,0:T(8,128)(2,1)S(1)}, bf16[1,128,128]{2,1,0:T(8,128)(2,1)S(1)}, u32[]{:S(2)}, u32[]{:S(2)}) collective-permute-start(bf16[1,128,128]{2,1,0:T(8,128)(2,1)S(1)} %get-tuple-element.26), channel_id=1, source_target_pairs={{1,0},{2,1},{3,2},{4,3},{5,4},{6,5},{7,6},{9,8},{10,9},{11,10},{12... | collective-permute-start | bytes 98312 | tf_op jit(solution)/shard_map/ppermute | solution.py:17
  145.6 172.4 %copy-start.6 = (bf16[1,1,128,32]{2,3,1,0:T(8,128)(2,1)S(1)}, bf16[1,1,128,32]{2,3,1,0:T(8,128)(2,1)}, u32[]{:S(2)}) copy-start(bf16[1,1,128,32]{2,3,1,0:T(8,128)(2,1)} %param.13) | copy-start | bytes 24580
  318.0 22.1 %copy-start.4 = (f32[1,1,4,128]{3,2,1,0:T(4,128)S(1)}, f32[1,1,4,128]{3,2,1,0:T(4,128)}, u32[]{:S(2)}) copy-start(f32[1,1,4,128]{3,2,1,0:T(4,128)} %param.10) | copy-start | bytes 6148
  318.0 24.5 %copy-start.3 = (bf16[1,1,1,128,128]{4,3,2,1,0:T(8,128)(2,1)S(1)}, bf16[1,1,1,128,128]{4,3,2,1,0:T(8,128)(2,1)}, u32[]{:S(2)}) copy-start(bf16[1,1,1,128,128]{4,3,2,1,0:T(8,128)(2,1)} %param.11) | copy-start | bytes 98308
  326.6 10.2 collective-permute-start.4
  329.8 7.0 collective-permute-start.6
  333.6 5.2 collective-permute-start.5
  334.9 5.2 collective-permute-start.7
  546.8 201.0 %all-to-all-start.1 = ((bf16[512,32,128]{2,1,0:T(8,128)(2,1)}), bf16[512,32,128]{2,1,0:T(8,128)(2,1)}, u32[]{:S(2)}, u32[]{:S(2)}) async-start(bf16[512,32,128]{2,1,0:T(8,128)(2,1)} %stack.16), calls=%async_computation.1 | async-start | bytes 8388608 | tf_op jit(solution)/shard_map/all_to_all | solution.py:82
  561.4 10.2 collective-permute-start.8
  564.7 6.9 collective-permute-start.10
  568.3 5.2 collective-permute-start.9
  569.6 5.9 collective-permute-start.11
  756.4 10.2 collective-permute-start.12
  759.6 7.0 collective-permute-start.14
  763.3 5.2 collective-permute-start.13
  764.6 5.2 collective-permute-start.15
